TPU v7x, 512 devices: a whole 4x4x16 slice. The times are simulated.
512 devices in a mesh: pipe: 32 (over z, x_hi), tensor: 16 (over x_lo, y, core).
Axes of the slice: x: 4 (x_hi: 2, x_lo: 2; x = x_hi * 2 + x_lo), y: 4, z: 16, core: 2. Of those that a mesh axis runs over, the one named last changes fastest.
Arguments:
- x_saved: bfloat16 [32, 2, 4096, 128], P('pipe', None, 'tensor'), may hold values from -6 to 6
- seed_grad: bfloat16 [32, 2, 4096, 128], P('pipe', None, 'tensor'), may hold values from -6 to 6
- gate_blocks: bfloat16 [32, 16, 7, 20, 4096], P('pipe', 'tensor'), may hold values from -0.1875 to 0.1875
- up_blocks: bfloat16 [32, 16, 7, 20, 4096], P('pipe', 'tensor'), may hold values from -0.1875 to 0.1875
- down_blocks: bfloat16 [32, 16, 7, 20, 4096], P('pipe', 'tensor'), may hold values from -0.1875 to 0.1875
- gate_rows: int32 [32, 16, 7, 20], P('pipe', 'tensor'), may hold values from -1 to 63, as said below
- down_rows: int32 [32, 16, 7, 20], P('pipe', 'tensor'), may hold values from -1 to 63, as said below
Outputs:
- grad_input: bfloat16 [32, 2, 4096, 128], P('pipe', None, 'tensor')
Inputs may be any that keep to these rules, and one draw needn't show every extreme that they name: `gate_rows`: in one column of tiles the non-negative entries are distinct and come before the -1 entries. All columns of one tensor shard of one section hold the same number of kept tiles, from 12 to 20, and in every section one shard holds 20 in every column. `down_rows`: as for gate_rows, drawn independently.
All inputs are finite; a program needn't handle non-finite values.
Results may differ from a plain program's by a relative error of at most 0.007.
Values may be sent and summed in bfloat16 or wider, within the bound.
No kernel may reach another device: no remote copies, remote signals or barrier semaphores. Data moves between devices by JAX's collectives and lax.ppermute only.
A program may use at most 128 MiB of HBM per device.

v0:
```python
import jax
import jax.numpy as jnp
from jax import lax
from jax.sharding import PartitionSpec as P

BLK = 64


def partner_2(x, axis, distance):
    return lax.ppermute(x, axis, [(i, i ^ 1 << distance) for i in range(lax.axis_size(axis))])


def from_behind(block, axis, distance):
    devices = range(lax.axis_size(axis))
    route = [(i - distance, i) for i in devices if i - distance in devices]
    return lax.ppermute(block, axis, route)


def gather_tiles(source, row_ids):
    columns, slot_depth = row_ids.shape
    filled = (row_ids >= 0).reshape(-1)
    picked = jnp.take(source, jnp.maximum(row_ids, 0).reshape(-1), axis=0)
    picked = jnp.where(filled[:, None, None], picked, jnp.zeros_like(picked))
    return picked.reshape(columns, slot_depth, source.shape[1], source.shape[2])


def layer_branch(x_full, cot_full, paired_grid, down_grid, gate_ids, down_ids):
    row_blocks = x_full.shape[0] // BLK
    tokens_now = x_full.shape[1]
    columns, slot_depth = gate_ids.shape
    x_picked = gather_tiles(x_full.reshape(row_blocks, BLK, tokens_now), gate_ids)
    both_values = jnp.einsum(
        "crkj,crkt->cjt", paired_grid, x_picked, preferred_element_type=jnp.float32
    )
    gate_value = both_values[:, :BLK]
    up_value = both_values[:, BLK:]
    cot_picked = gather_tiles(cot_full.reshape(row_blocks, BLK, tokens_now), down_ids)
    d_hidden = jnp.einsum(
        "crjk,crkt->cjt", down_grid, cot_picked, preferred_element_type=jnp.float32
    )
    sigmoid_gate = jax.nn.sigmoid(gate_value)
    d_gate = (
        d_hidden * up_value * sigmoid_gate * (1.0 + gate_value * (1.0 - sigmoid_gate))
    ).astype(jnp.bfloat16)
    d_up = (d_hidden * gate_value * sigmoid_gate).astype(jnp.bfloat16)
    d_both = jnp.concatenate([d_gate, d_up], axis=1)
    per_slot = jnp.einsum("crkj,cjt->crkt", paired_grid, d_both, preferred_element_type=jnp.float32)
    segment_ids = jnp.where(gate_ids >= 0, gate_ids, row_blocks).reshape(-1)
    summed = jax.ops.segment_sum(
        per_slot.reshape(columns * slot_depth, BLK, tokens_now),
        segment_ids,
        num_segments=row_blocks + 1,
    )
    return summed[:row_blocks].reshape(row_blocks * BLK, tokens_now)


def per_device(x_saved, seed_grad, gate_blocks, up_blocks, down_blocks, gate_rows, down_rows):
    pipe_index = lax.axis_index("pipe")
    pair_half = pipe_index % 2
    last_section = pipe_index // 2 == lax.axis_size("pipe") // 2 - 1
    own_parts = (gate_blocks, up_blocks, down_blocks, gate_rows, down_rows)
    partner = partner_2((gate_blocks, up_blocks, down_blocks, gate_rows, down_rows), "pipe", 0)
    joined = []
    for own_part, theirs in zip(own_parts, partner):
        first_half = jnp.where(pair_half == 0, own_part, theirs)
        second_half = jnp.where(pair_half == 0, theirs, own_part)
        joined.append(jnp.concatenate([first_half[0, 0], second_half[0, 0]], axis=0))
    gate_set, up_set, down_set, gate_ids, down_ids = joined
    columns, slot_depth = gate_ids.shape
    tile_shape = (columns, slot_depth, BLK, BLK)
    paired_grid = jnp.concatenate(
        [gate_set.reshape(tile_shape), up_set.reshape(tile_shape)], axis=3
    )
    down_grid = down_set.reshape(tile_shape)
    panel_rows = x_saved.shape[2]
    micro_total = x_saved.shape[1]
    arrived = None
    grads = []
    for micro_step in range(micro_total):
        x_panel = x_saved[0, micro_step]
        seed_panel = seed_grad[0, micro_step]
        x_full, cot_full = (
            lax.all_gather(x_panel, "tensor", axis=0, tiled=True),
            lax.all_gather(seed_panel, "tensor", axis=0, tiled=True),
        )
        if micro_step > 0:
            cot_full = jnp.where(last_section, cot_full, arrived)
        branch = layer_branch(x_full, cot_full, paired_grid, down_grid, gate_ids, down_ids)
        summed = lax.psum(branch, "tensor")
        grad_full = (cot_full.astype(jnp.float32) + summed).astype(jnp.bfloat16)
        grad_panel = lax.dynamic_slice_in_dim(
            grad_full, lax.axis_index("tensor") * panel_rows, panel_rows, 0
        )
        if micro_step + 1 < micro_total:
            arrived = from_behind(grad_full, "pipe", -2)
        grads.append(grad_panel)
    return jnp.stack(grads)[None]


def solution(mesh):
    return jax.shard_map(
        per_device,
        mesh=mesh,
        in_specs=(
            P("pipe", None, "tensor", None),
            P("pipe", None, "tensor", None),
            P("pipe", "tensor", None, None, None),
            P("pipe", "tensor", None, None, None),
            P("pipe", "tensor", None, None, None),
            P("pipe", "tensor", None, None),
            P("pipe", "tensor", None, None),
        ),
        out_specs=P("pipe", None, "tensor", None),
        check_vma=False,
    )
```

profile of v0, /device:TPU:1, one launch (start us, length us, event | category | flops | bytes accessed | tf_op | source)
XLA Modules:
  0.0 603.3 jit_solution(8425488830314063497)
XLA Ops:
  9.6 5.5 collective-permute-start
  17.0 4.9 collective-permute-start.3
  23.8 4.9 collective-permute-start.1
  31.7 19.6 %collective-permute-done.3 = bf16[1,1,7,20,4096]{4,2,3,1,0:T(8,128)(2,1)S(1)} collective-permute-done((bf16[1,1,7,20,4096]{4,2,3,1,0:T(8,128)(2,1)}, bf16[1,1,7,20,4096]{4,2,3,1,0:T(8,128)(2,1)S(1)}, u32[]{:S(2)}, u32[]{:S(2)}) %collective-permute-start.3) | collective-permute-done | bytes 1146912 | tf_op jit(solution)/shard_map/ppermute | solution.py:10
  51.3 29.8 %collective-permute-done.2 = bf16[1,1,7,20,4096]{4,2,3,1,0:T(8,128)(2,1)S(1)} collective-permute-done((bf16[1,1,7,20,4096]{4,2,3,1,0:T(8,128)(2,1)}, bf16[1,1,7,20,4096]{4,2,3,1,0:T(8,128)(2,1)S(1)}, u32[]{:S(2)}, u32[]{:S(2)}) %collective-permute-start.2) | collective-permute-done | bytes 1146912 | tf_op jit(solution)/shard_map/ppermute | solution.py:10
  89.0 4.5 concatenate.46
  93.5 19.2 %collective-permute-done.1 = bf16[1,1,7,20,4096]{4,2,3,1,0:T(8,128)(2,1)} collective-permute-done((bf16[1,1,7,20,4096]{4,2,3,1,0:T(8,128)(2,1)}, bf16[1,1,7,20,4096]{4,2,3,1,0:T(8,128)(2,1)}, u32[]{:S(2)}, u32[]{:S(2)}) %collective-permute-start.1) | collective-permute-done | bytes 1146912 | tf_op jit(solution)/shard_map/ppermute | solution.py:10
  116.1 4.5 concatenate.44
  134.2 6.4 %maximum_maximum_fusion = bf16[14,20,64,128]{3,2,0,1:T(8,128)(2,1)} fusion(bf16[7,20,64,64]{3,2,0,1:T(8,128)(2,1)S(1)} %concatenate.47, bf16[7,20,64,64]{3,2,0,1:T(8,128)(2,1)} %concatenate.46, bf16[7,20,64,64]{3,2,0,1:T(8,128)(2,1)} %concatenate.44, bf16[7,20,64,64]{3,2,0,1:T(8,128)(2,1)} %concatenate.43), kind=kLoop, calls=%fused_computation.6 | loop fusion | flops 18350080 | bytes 9175040 | tf_op jit(solution)/shard_map/concatenate | solution.py:71
  140.6 4.6 gather_fusion.3
  145.2 4.7 gather_fusion.1
  149.9 7.8 %select_select_fusion = (bf16[280,64,128]{2,1,0:T(8,128)(2,1)}, bf16[280,64,128]{2,1,0:T(8,128)(2,1)S(1)}) fusion(bf16[280,64,128]{2,1,0:T(8,128)(2,1)} %gather_fusion.3, pred[280]{0:T(512)(128)(4,1)S(1)} %compare_and_fusion, pred[280]{0:T(512)(128)(4,1)S(1)} %ge.42, bf16[280,64,128]{2,1,0:T(8,128)(2,1)} %gather_fusion.1), kind=kLoop, calls=%fused_computation.8 | loop fusion | flops 9175040 | bytes 18350640 | tf_op jit(solution)/shard_map/jit(_where)/select_n | solution.py:23
  159.3 4.7 gather_fusion
  164.0 4.7 select_select_fusion.3
  170.7 4.9 fusion.8
  175.9 29.8 %scatter_fusion = f32[65,64,128]{2,1,0:T(8,128)S(1)} fusion(f32[65,64,128]{2,1,0:T(8,128)S(1)} %broadcast.48.clone, s32[280]{0:T(512)S(1)} %fusion.40, f32[280,64,128]{2,1,0:T(8,128)} %bitcast.77), kind=kCustom, calls=%fused_computation.4 | custom fusion | flops 2293760 | bytes 27526240 | tf_op jit(solution)/shard_map/scatter-add | solution.py:49
  207.9 147.0 %all-reduce.3.cloned.1.call-done = f32[4096,128]{1,0:T(8,128)} async-done(((f32[4096,128]{1,0:T(8,128)}), f32[4096,128]{1,0:T(8,128)}) %all-reduce.3.cloned.1.call-update) | async-done | bytes 2097168 | tf_op jit(solution)/shard_map/psum | solution.py:89
  358.0 6.1 %fusion.16 = f32[14,128,128]{2,1,0:T(8,128)} fusion(bf16[14,20,64,128]{3,2,1,0:T(8,128)(2,1)} %bitcast.84, bf16[14,20,64,128]{3,2,0,1:T(8,128)(2,1)} %maximum_maximum_fusion), kind=kOutput, calls=%fused_computation.27 | convolution fusion | flops 587202560 | bytes 10092544 | tf_op jit(solution)/shard_map/crkj,crkt->cjt/dot_general | solution.py:32
  364.1 34.7 %all-gather.13.cloned.1.call-done = bf16[1,1,4096,128]{3,2,1,0:T(8,128)(2,1)} async-done(((bf16[1,1,256,128]{3,2,1,0:T(8,128)(2,1)}), bf16[1,1,4096,128]{3,2,1,0:T(8,128)(2,1)}) %all-gather.13.cloned.1.call-update) | async-done | bytes 1048592 | tf_op jit(solution)/shard_map/all_gather | solution.py:84
  400.1 13.6 %gather_fusion.2 = bf16[280,64,128]{2,1,0:T(8,128)(2,1)} fusion(bf16[64,64,128]{2,1,0:T(8,128)(2,1)S(1)} %bitcast.78, s32[1024]{0:T(1024)S(1)} %pad_clamp_fusion.1), kind=kCustom, calls=%fused_computation.2.clone | custom fusion | bytes 9176160 | tf_op jit(solution)/shard_map/jit(_take)/gather | solution.py:22
  413.7 4.7 select_select_fusion.1
  420.5 4.9 fusion.4
  425.7 29.8 %scatter_fusion.1 = f32[65,64,128]{2,1,0:T(8,128)S(1)} fusion(f32[65,64,128]{2,1,0:T(8,128)S(1)} %broadcast.48, s32[280]{0:T(512)S(1)} %fusion.40, f32[280,64,128]{2,1,0:T(8,128)} %bitcast.76), kind=kCustom, calls=%fused_computation.5 | custom fusion | flops 2293760 | bytes 27526240 | tf_op jit(solution)/shard_map/scatter-add | solution.py:49
  457.9 137.0 %all-reduce.5.cloned.1.call-done = f32[4096,128]{1,0:T(8,128)} async-done(((f32[4096,128]{1,0:T(8,128)}), f32[4096,128]{1,0:T(8,128)}) %all-reduce.5.cloned.1.call-update) | async-done | bytes 2097168 | tf_op jit(solution)/shard_map/psum | solution.py:89
  (90 shorter events, 51.0 us)
Async XLA Ops:
  6.5 134.1 %all-gather.15.cloned.1.call-start = ((), (), s32[]{:S(2)}) async-start(), calls=%async_computation.5 | async-start | bytes 1114112 | tf_op jit(solution)/shard_map/all_gather | solution.py:83
  8.1 137.1 %all-gather.11.cloned.1.call-start = ((), (), s32[]{:S(2)}) async-start(), calls=%async_computation.3 | async-start | bytes 1114112 | tf_op jit(solution)/shard_map/all_gather | solution.py:83
  8.8 150.5 %all-gather.9.cloned.1.call-start = ((), (), s32[]{:S(2)}) async-start(), calls=%async_computation.2 | async-start | bytes 1114112 | tf_op jit(solution)/shard_map/all_gather | solution.py:84
  9.6 20.7 %collective-permute-start = (s32[1,1,7,20]{3,2,1,0:T(8,128)S(1)}, s32[1,1,7,20]{3,2,1,0:T(8,128)S(1)}, u32[]{:S(2)}, u32[]{:S(2)}) collective-permute-start(s32[1,1,7,20]{3,2,1,0:T(8,128)S(1)} %copy.21), channel_id=1, source_target_pairs={{0,16},{16,0},{32,48},{48,32},{64,80},{80,64},{96,112},{112,96},{1... | collective-permute-start | bytes 1688 | tf_op jit(solution)/shard_map/ppermute | solution.py:10
  15.1 15.3 %collective-permute-start.4 = (s32[1,1,7,20]{3,1,2,0:T(1,128)}, s32[1,1,7,20]{3,1,2,0:T(1,128)S(1)}, u32[]{:S(2)}, u32[]{:S(2)}) collective-permute-start(s32[1,1,7,20]{3,1,2,0:T(1,128)} %param.15), channel_id=1, source_target_pairs={{0,16},{16,0},{32,48},{48,32},{64,80},{80,64},{96,112},{112,96},{1... | collective-permute-start | bytes 1688 | tf_op jit(solution)/shard_map/ppermute | solution.py:10
  17.0 34.3 %collective-permute-start.3 = (bf16[1,1,7,20,4096]{4,2,3,1,0:T(8,128)(2,1)}, bf16[1,1,7,20,4096]{4,2,3,1,0:T(8,128)(2,1)S(1)}, u32[]{:S(2)}, u32[]{:S(2)}) collective-permute-start(bf16[1,1,7,20,4096]{4,2,3,1,0:T(8,128)(2,1)} %param.13), channel_id=1, source_target_pairs={{0,16},{16,0},{32,48},{48,32},{64,80},{80,64},{96,112},{112,96},{1... | collective-permute-start | bytes 3440648 | tf_op jit(solution)/shard_map/ppermute | solution.py:10
  21.9 59.2 %collective-permute-start.2 = (bf16[1,1,7,20,4096]{4,2,3,1,0:T(8,128)(2,1)}, bf16[1,1,7,20,4096]{4,2,3,1,0:T(8,128)(2,1)S(1)}, u32[]{:S(2)}, u32[]{:S(2)}) collective-permute-start(bf16[1,1,7,20,4096]{4,2,3,1,0:T(8,128)(2,1)} %param.12), channel_id=1, source_target_pairs={{0,16},{16,0},{32,48},{48,32},{64,80},{80,64},{96,112},{112,96},{1... | collective-permute-start | bytes 3440648 | tf_op jit(solution)/shard_map/ppermute | solution.py:10
  23.8 88.9 %collective-permute-start.1 = (bf16[1,1,7,20,4096]{4,2,3,1,0:T(8,128)(2,1)}, bf16[1,1,7,20,4096]{4,2,3,1,0:T(8,128)(2,1)}, u32[]{:S(2)}, u32[]{:S(2)}) collective-permute-start(bf16[1,1,7,20,4096]{4,2,3,1,0:T(8,128)(2,1)} %param.11), channel_id=1, source_target_pairs={{0,16},{16,0},{32,48},{48,32},{64,80},{80,64},{96,112},{112,96},{1... | collective-permute-start | bytes 3440648 | tf_op jit(solution)/shard_map/ppermute | solution.py:10
  30.2 324.6 %all-reduce.3.cloned.1.call-start = ((), (), s32[]{:S(2)}) async-start(), calls=%async_computation | async-start | bytes 4194304 | tf_op jit(solution)/shard_map/psum | solution.py:89
  145.2 12.5 %slice-start = ((s8[4587520]{0:T(1024)(128)(4,1)}), s8[393216]{0:T(1024)(128)(4,1)S(1)}, s32[]{:S(2)}) async-start(s8[4587520]{0:T(1024)(128)(4,1)} %bitcast.70), calls=%async_computation.6 | async-start | bytes 786432
  149.9 7.8 %slice-start.1 = ((s8[4587520]{0:T(1024)(128)(4,1)}), s8[4194304]{0:T(1024)(128)(4,1)S(1)}, s32[]{:S(2)}) async-start(s8[4587520]{0:T(1024)(128)(4,1)} %bitcast.70), calls=%async_computation.7 | async-start | bytes 8388608
  163.9 4.7 copy-start.1
  164.0 4.7 copy-start.3
  164.0 6.8 %slice-start.2 = ((s8[4587520]{0:T(1024)(128)(4,1)}), s8[4194304]{0:T(1024)(128)(4,1)S(1)}, s32[]{:S(2)}) async-start(s8[4587520]{0:T(1024)(128)(4,1)} %bitcast.72), calls=%async_computation.8 | async-start | bytes 8388608
  168.7 2.0 slice-start.3
  205.7 149.1 %copy-start = (bf16[1,1,4096,128]{3,2,1,0:T(8,128)(2,1)S(1)}, bf16[1,1,4096,128]{3,2,1,0:T(8,128)(2,1)}, u32[]{:S(2)}) copy-start(bf16[1,1,4096,128]{3,2,1,0:T(8,128)(2,1)} %all-gather.9.cloned.1.call-done) | copy-start | bytes 3145732
  207.2 191.6 %all-gather.13.cloned.1.call-start = ((), (), s32[]{:S(2)}) async-start(), calls=%async_computation.4 | async-start | bytes 1114112 | tf_op jit(solution)/shard_map/all_gather | solution.py:84
  207.8 387.0 %all-reduce.5.cloned.1.call-start = ((), (), s32[]{:S(2)}) async-start(), calls=%async_computation.1 | async-start | bytes 4194304 | tf_op jit(solution)/shard_map/psum | solution.py:89
  356.7 7.4 %copy-start.5 = (bf16[4096,128]{1,0:T(8,128)(2,1)}, bf16[4096,128]{1,0:T(8,128)(2,1)S(1)}, u32[]{:S(2)}) copy-start(bf16[4096,128]{1,0:T(8,128)(2,1)S(1)} %fusion.12) | copy-start | bytes 3145732
  356.7 42.1 %collective-permute-start.5 = (bf16[4096,128]{1,0:T(8,128)(2,1)S(1)}, bf16[4096,128]{1,0:T(8,128)(2,1)S(1)}, u32[]{:S(2)}, u32[]{:S(2)}) collective-permute-start(bf16[4096,128]{1,0:T(8,128)(2,1)S(1)} %fusion.12), channel_id=1, source_target_pairs={{32,0},{48,16},{64,32},{80,48},{96,64},{112,80},{128,96},{144,112}... | collective-permute-start | bytes 3145736 | tf_op jit(solution)/shard_map/ppermute | solution.py:16
  400.1 18.3 %copy-start.6 = (f32[14,128,128]{2,1,0:T(8,128)S(1)}, f32[14,128,128]{2,1,0:T(8,128)}, u32[]{:S(2)}) copy-start(f32[14,128,128]{2,1,0:T(8,128)} %fusion.16) | copy-start | bytes 2752516
  413.7 4.8 copy-start.2
  413.7 4.8 copy-start.4
  413.7 6.8 %slice-start.4 = ((s8[4587520]{0:T(1024)(128)(4,1)}), s8[4194304]{0:T(1024)(128)(4,1)S(1)}, s32[]{:S(2)}) async-start(s8[4587520]{0:T(1024)(128)(4,1)} %bitcast.74), calls=%async_computation.10 | async-start | bytes 8388608
  (1 other events, 2.0 us)
Sparse Core Ops, SparseCore 0:
  9.5 47.1 all-gather.14
  58.9 41.6 all-gather.10
  102.7 40.2 all-gather.8
  207.3 147.4 all-reduce.2
  356.8 41.8 all-gather.12
  457.1 137.6 all-reduce.4
where the time goes:
time: 606 us; the launch traced here: 603 us
  waiting for transfers between devices  389 us (64%)
  other arithmetic  96.3 us (16%)
  local copies, waits for them, and re-layouts  62.3 us (10%)
  matrix products  21.5 us (4%)
  starting transfers between devices  20.5 us (3%)
  between operations  14 us (2%)
    psum x2, waiting for transfers between devices, per_device(): summed = lax.psum(branch, 'tensor')  284 us
    ppermute x5, waiting for transfers between devices, partner_2(): lax.ppermute(x, axis, [(i, i ^ 1 << distance) for i in range(lax.axis_siz...  68.6 us
    scatter-add x2, other arithmetic, layer_branch(): jax.ops.segment_sum(per_slot.reshape(columns * slot_depth, BLK, tokens_no...  59.5 us
    all_gather x2, waiting for transfers between devices, per_device(): lax.all_gather(seed_panel, 'tensor', axis=0, tiled=True)  34.7 us
    gather x4, local copies, waits for them, and re-layouts, gather_tiles(): picked = jnp.take(source, jnp.maximum(row_ids, 0).reshape(-1), axis=0)  27.5 us
    concatenate x7, local copies, waits for them, and re-layouts, per_device(): jnp.concatenate([first_half[0, 0], second_half[0, 0]], axis=0)  26.4 us
    ppermute x5, starting transfers between devices, partner_2(): lax.ppermute(x, axis, [(i, i ^ 1 << distance) for i in range(lax.axis_siz...  19.1 us
    select_n x3, other arithmetic, gather_tiles(): picked = jnp.where(filled[:, None, None], picked, jnp.zeros_like(picked))  17.3 us
  transfers between devices with their start and end apart: 12, of which 6 were waited for; matrix products, arithmetic and copies ran while one was open for 12% of the time, Pallas kernels for 0%

commit v1 on v0

--- a/solution.py
+++ b/solution.py
@@ -86,7 +86,7 @@
         if micro_step > 0:
             cot_full = jnp.where(last_section, cot_full, arrived)
         branch = layer_branch(x_full, cot_full, paired_grid, down_grid, gate_ids, down_ids)
-        summed = lax.psum(branch, "tensor")
+        summed = jnp.sum(lax.all_gather(branch, "tensor"), axis=0)
         grad_full = (cot_full.astype(jnp.float32) + summed).astype(jnp.bfloat16)
         grad_panel = lax.dynamic_slice_in_dim(
             grad_full, lax.axis_index("tensor") * panel_rows, panel_rows, 0

time: 606 us -> 697 us (1.15)
  waiting for transfers between devices: 389 us -> 459 us
  other arithmetic: 96.3 us -> 118 us
    all_gather x0 -> x2, waiting for transfers between devices: none -> 365 us  [per_device(): summed = jnp.sum(lax.all_gather(branch, 'tensor'), axis=0)]
    psum x2 -> x0, waiting for transfers between devices: 284 us -> none  [per_device(): summed = lax.psum(branch, 'tensor')]
    reduce_sum x0 -> x2, other arithmetic: none -> 23.5 us  [per_device(): summed = jnp.sum(lax.all_gather(branch, 'tensor'), axis=0)]
    all_gather x2, waiting for transfers between devices: 34.7 us -> 23.8 us  [per_device(): lax.all_gather(seed_panel, 'tensor', axis=0, tiled=True)]
where the time goes in v1:
time: 697 us; the launch traced here: 694 us
  waiting for transfers between devices  459 us (66%)
  other arithmetic  118 us (17%)
  local copies, waits for them, and re-layouts  62.2 us (9%)
  starting transfers between devices  20.5 us (3%)
  matrix products  20.5 us (3%)
  between operations  14 us (2%)
    all_gather x2, waiting for transfers between devices, per_device(): summed = jnp.sum(lax.all_gather(branch, 'tensor'), axis=0)  365 us
    ppermute x5, waiting for transfers between devices, partner_2(): lax.ppermute(x, axis, [(i, i ^ 1 << distance) for i in range(lax.axis_siz...  68.7 us
    scatter-add x2, other arithmetic, layer_branch(): jax.ops.segment_sum(per_slot.reshape(columns * slot_depth, BLK, tokens_no...  59.5 us
    gather x4, local copies, waits for them, and re-layouts, gather_tiles(): picked = jnp.take(source, jnp.maximum(row_ids, 0).reshape(-1), axis=0)  27.5 us
    concatenate x7, local copies, waits for them, and re-layouts, per_device(): jnp.concatenate([first_half[0, 0], second_half[0, 0]], axis=0)  26.3 us
    all_gather x2, waiting for transfers between devices, per_device(): lax.all_gather(seed_panel, 'tensor', axis=0, tiled=True)  23.8 us
    reduce_sum x2, other arithmetic, per_device(): summed = jnp.sum(lax.all_gather(branch, 'tensor'), axis=0)  23.5 us
    ppermute x5, starting transfers between devices, partner_2(): lax.ppermute(x, axis, [(i, i ^ 1 << distance) for i in range(lax.axis_siz...  19.1 us
  transfers between devices with their start and end apart: 12, of which 6 were waited for; matrix products, arithmetic and copies ran while one was open for 12% of the time, Pallas kernels for 0%

profile of v1, /device:TPU:1, one launch (start us, length us, event | category | flops | bytes accessed | tf_op | source)
XLA Modules:
  0.0 694.4 jit_solution(15825447096296014825)
XLA Ops:
  9.6 5.5 collective-permute-start
  17.0 4.9 collective-permute-start.3
  23.8 4.9 collective-permute-start.1
  31.7 19.6 %collective-permute-done.3 = bf16[1,1,7,20,4096]{4,2,3,1,0:T(8,128)(2,1)S(1)} collective-permute-done((bf16[1,1,7,20,4096]{4,2,3,1,0:T(8,128)(2,1)}, bf16[1,1,7,20,4096]{4,2,3,1,0:T(8,128)(2,1)S(1)}, u32[]{:S(2)}, u32[]{:S(2)}) %collective-permute-start.3) | collective-permute-done | bytes 1146912 | tf_op jit(solution)/shard_map/ppermute | solution.py:10
  51.3 29.8 %collective-permute-done.2 = bf16[1,1,7,20,4096]{4,2,3,1,0:T(8,128)(2,1)S(1)} collective-permute-done((bf16[1,1,7,20,4096]{4,2,3,1,0:T(8,128)(2,1)}, bf16[1,1,7,20,4096]{4,2,3,1,0:T(8,128)(2,1)S(1)}, u32[]{:S(2)}, u32[]{:S(2)}) %collective-permute-start.2) | collective-permute-done | bytes 1146912 | tf_op jit(solution)/shard_map/ppermute | solution.py:10
  93.5 19.2 %collective-permute-done.1 = bf16[1,1,7,20,4096]{4,2,3,1,0:T(8,128)(2,1)} collective-permute-done((bf16[1,1,7,20,4096]{4,2,3,1,0:T(8,128)(2,1)}, bf16[1,1,7,20,4096]{4,2,3,1,0:T(8,128)(2,1)}, u32[]{:S(2)}, u32[]{:S(2)}) %collective-permute-start.1) | collective-permute-done | bytes 1146912 | tf_op jit(solution)/shard_map/ppermute | solution.py:10
  134.2 6.4 maximum_maximum_fusion
  140.5 4.6 gather_fusion.3
  145.2 4.7 gather_fusion.1
  149.9 7.8 %select_select_fusion = (bf16[280,64,128]{2,1,0:T(8,128)(2,1)}, bf16[280,64,128]{2,1,0:T(8,128)(2,1)S(1)}) fusion(bf16[280,64,128]{2,1,0:T(8,128)(2,1)} %gather_fusion.3, pred[280]{0:T(512)(128)(4,1)S(1)} %compare_and_fusion, pred[280]{0:T(512)(128)(4,1)S(1)} %ge.42, bf16[280,64,128]{2,1,0:T(8,128)(2,1)} %gather_fusion.1), kind=kLoop, calls=%fused_computation.8 | loop fusion | flops 9175040 | bytes 18350640 | tf_op jit(solution)/shard_map/jit(_where)/select_n | solution.py:23
  159.2 4.6 gather_fusion
  163.9 4.7 select_select_fusion.3
  170.7 4.9 fusion.8
  175.8 29.8 %scatter_fusion = f32[65,64,128]{2,1,0:T(8,128)S(1)} fusion(f32[65,64,128]{2,1,0:T(8,128)S(1)} %broadcast.48.clone, s32[280]{0:T(512)S(1)} %fusion.40, f32[280,64,128]{2,1,0:T(8,128)} %bitcast.77), kind=kCustom, calls=%fused_computation.4 | custom fusion | flops 2293760 | bytes 27526240 | tf_op jit(solution)/shard_map/scatter-add | solution.py:49
  207.7 187.6 %all-gather.11.cloned.1.call-done = f32[16,4096,128]{2,1,0:T(8,128)} async-done(((f32[1,4096,128]{2,1,0:T(8,128)}), f32[16,4096,128]{2,1,0:T(8,128)}) %all-gather.11.cloned.1.call-update) | async-done | bytes 33554448 | tf_op jit(solution)/shard_map/all_gather | solution.py:89
  395.3 11.7 %reduce_sum.18 = f32[4096,128]{1,0:T(8,128)S(1)} reduce(f32[16,4096,128]{2,1,0:T(8,128)} %all-gather.11.cloned.1.call-done, f32[]{:T(128)} %constant.26.clone.1), dimensions={0}, to_apply=%region_1.3 | reduce | flops 7864320 | bytes 35651588 | tf_op jit(solution)/shard_map/reduce_sum | solution.py:89
  409.6 5.1 fusion.16
  414.7 23.8 %all-gather.19.cloned.1.call-done = bf16[1,1,4096,128]{3,2,1,0:T(8,128)(2,1)} async-done(((bf16[1,1,256,128]{3,2,1,0:T(8,128)(2,1)}), bf16[1,1,4096,128]{3,2,1,0:T(8,128)(2,1)}) %all-gather.19.cloned.1.call-update) | async-done | bytes 1048592 | tf_op jit(solution)/shard_map/all_gather | solution.py:84
  439.8 13.6 %gather_fusion.2 = bf16[280,64,128]{2,1,0:T(8,128)(2,1)} fusion(bf16[64,64,128]{2,1,0:T(8,128)(2,1)S(1)} %bitcast.78, s32[1024]{0:T(1024)S(1)} %pad_clamp_fusion.1), kind=kCustom, calls=%fused_computation.2.clone | custom fusion | bytes 9176160 | tf_op jit(solution)/shard_map/jit(_take)/gather | solution.py:22
  453.4 4.7 select_select_fusion.1
  460.2 4.9 fusion.4
  465.4 29.8 %scatter_fusion.1 = f32[65,64,128]{2,1,0:T(8,128)S(1)} fusion(f32[65,64,128]{2,1,0:T(8,128)S(1)} %broadcast.48, s32[280]{0:T(512)S(1)} %fusion.40, f32[280,64,128]{2,1,0:T(8,128)} %bitcast.76), kind=kCustom, calls=%fused_computation.5 | custom fusion | flops 2293760 | bytes 27526240 | tf_op jit(solution)/shard_map/scatter-add | solution.py:49
  497.5 177.6 %all-gather.13.cloned.1.call-done = f32[16,4096,128]{2,1,0:T(8,128)} async-done(((f32[1,4096,128]{2,1,0:T(8,128)}), f32[16,4096,128]{2,1,0:T(8,128)}) %all-gather.13.cloned.1.call-update) | async-done | bytes 33554448 | tf_op jit(solution)/shard_map/all_gather | solution.py:89
  675.1 11.7 %reduce_sum.19 = f32[4096,128]{1,0:T(8,128)S(1)} reduce(f32[16,4096,128]{2,1,0:T(8,128)} %all-gather.13.cloned.1.call-done, f32[]{:T(128)} %constant.26.clone.1), dimensions={0}, to_apply=%region_3.5 | reduce | flops 7864320 | bytes 35651588 | tf_op jit(solution)/shard_map/reduce_sum | solution.py:89
  (88 shorter events, 58.5 us)
Async XLA Ops:
  6.5 134.0 %all-gather.21.cloned.1.call-start = ((), (), s32[]{:S(2)}) async-start(), calls=%async_computation.5 | async-start | bytes 1114112 | tf_op jit(solution)/shard_map/all_gather | solution.py:83
  8.1 137.1 %all-gather.17.cloned.1.call-start = ((), (), s32[]{:S(2)}) async-start(), calls=%async_computation.3 | async-start | bytes 1114112 | tf_op jit(solution)/shard_map/all_gather | solution.py:83
  8.8 150.4 %all-gather.15.cloned.1.call-start = ((), (), s32[]{:S(2)}) async-start(), calls=%async_computation.2 | async-start | bytes 1114112 | tf_op jit(solution)/shard_map/all_gather | solution.py:84
  9.6 20.7 %collective-permute-start = (s32[1,1,7,20]{3,2,1,0:T(8,128)S(1)}, s32[1,1,7,20]{3,2,1,0:T(8,128)S(1)}, u32[]{:S(2)}, u32[]{:S(2)}) collective-permute-start(s32[1,1,7,20]{3,2,1,0:T(8,128)S(1)} %copy.33), channel_id=1, source_target_pairs={{0,16},{16,0},{32,48},{48,32},{64,80},{80,64},{96,112},{112,96},{1... | collective-permute-start | bytes 1688 | tf_op jit(solution)/shard_map/ppermute | solution.py:10
  15.0 15.2 %collective-permute-start.4 = (s32[1,1,7,20]{3,1,2,0:T(1,128)}, s32[1,1,7,20]{3,1,2,0:T(1,128)S(1)}, u32[]{:S(2)}, u32[]{:S(2)}) collective-permute-start(s32[1,1,7,20]{3,1,2,0:T(1,128)} %param.15), channel_id=1, source_target_pairs={{0,16},{16,0},{32,48},{48,32},{64,80},{80,64},{96,112},{112,96},{1... | collective-permute-start | bytes 1688 | tf_op jit(solution)/shard_map/ppermute | solution.py:10
  17.0 34.3 %collective-permute-start.3 = (bf16[1,1,7,20,4096]{4,2,3,1,0:T(8,128)(2,1)}, bf16[1,1,7,20,4096]{4,2,3,1,0:T(8,128)(2,1)S(1)}, u32[]{:S(2)}, u32[]{:S(2)}) collective-permute-start(bf16[1,1,7,20,4096]{4,2,3,1,0:T(8,128)(2,1)} %param.13), channel_id=1, source_target_pairs={{0,16},{16,0},{32,48},{48,32},{64,80},{80,64},{96,112},{112,96},{1... | collective-permute-start | bytes 3440648 | tf_op jit(solution)/shard_map/ppermute | solution.py:10
  21.9 59.2 %collective-permute-start.2 = (bf16[1,1,7,20,4096]{4,2,3,1,0:T(8,128)(2,1)}, bf16[1,1,7,20,4096]{4,2,3,1,0:T(8,128)(2,1)S(1)}, u32[]{:S(2)}, u32[]{:S(2)}) collective-permute-start(bf16[1,1,7,20,4096]{4,2,3,1,0:T(8,128)(2,1)} %param.12), channel_id=1, source_target_pairs={{0,16},{16,0},{32,48},{48,32},{64,80},{80,64},{96,112},{112,96},{1... | collective-permute-start | bytes 3440648 | tf_op jit(solution)/shard_map/ppermute | solution.py:10
  23.8 88.9 %collective-permute-start.1 = (bf16[1,1,7,20,4096]{4,2,3,1,0:T(8,128)(2,1)}, bf16[1,1,7,20,4096]{4,2,3,1,0:T(8,128)(2,1)}, u32[]{:S(2)}, u32[]{:S(2)}) collective-permute-start(bf16[1,1,7,20,4096]{4,2,3,1,0:T(8,128)(2,1)} %param.11), channel_id=1, source_target_pairs={{0,16},{16,0},{32,48},{48,32},{64,80},{80,64},{96,112},{112,96},{1... | collective-permute-start | bytes 3440648 | tf_op jit(solution)/shard_map/ppermute | solution.py:10
  30.2 365.1 %all-gather.11.cloned.1.call-start = ((), (), s32[]{:S(2)}) async-start(), calls=%async_computation | async-start | bytes 35651584 | tf_op jit(solution)/shard_map/all_gather | solution.py:89
  145.2 12.5 %slice-start = ((s8[4587520]{0:T(1024)(128)(4,1)}), s8[393216]{0:T(1024)(128)(4,1)S(1)}, s32[]{:S(2)}) async-start(s8[4587520]{0:T(1024)(128)(4,1)} %bitcast.70), calls=%async_computation.6 | async-start | bytes 786432
  149.9 7.8 %slice-start.1 = ((s8[4587520]{0:T(1024)(128)(4,1)}), s8[4194304]{0:T(1024)(128)(4,1)S(1)}, s32[]{:S(2)}) async-start(s8[4587520]{0:T(1024)(128)(4,1)} %bitcast.70), calls=%async_computation.7 | async-start | bytes 8388608
  163.9 4.7 copy-start.1
  163.9 4.7 copy-start.3
  163.9 6.8 slice-start.2
  168.6 2.0 slice-start.3
  207.1 231.4 %all-gather.19.cloned.1.call-start = ((), (), s32[]{:S(2)}) async-start(), calls=%async_computation.4 | async-start | bytes 1114112 | tf_op jit(solution)/shard_map/all_gather | solution.py:84
  207.7 199.4 %copy-start = (bf16[1,1,4096,128]{3,2,1,0:T(8,128)(2,1)S(1)}, bf16[1,1,4096,128]{3,2,1,0:T(8,128)(2,1)}, u32[]{:S(2)}) copy-start(bf16[1,1,4096,128]{3,2,1,0:T(8,128)(2,1)} %all-gather.15.cloned.1.call-done) | copy-start | bytes 3145732
  207.7 467.5 %all-gather.13.cloned.1.call-start = ((), (), s32[]{:S(2)}) async-start(), calls=%async_computation.1 | async-start | bytes 35651584 | tf_op jit(solution)/shard_map/all_gather | solution.py:89
  408.3 30.2 %collective-permute-start.5 = (bf16[4096,128]{1,0:T(8,128)(2,1)}, bf16[4096,128]{1,0:T(8,128)(2,1)S(1)}, u32[]{:S(2)}, u32[]{:S(2)}) collective-permute-start(bf16[4096,128]{1,0:T(8,128)(2,1)} %fusion.12), channel_id=1, source_target_pairs={{32,0},{48,16},{64,32},{80,48},{96,64},{112,80},{128,96},{144,112}... | collective-permute-start | bytes 3145736 | tf_op jit(solution)/shard_map/ppermute | solution.py:16
  453.4 4.8 copy-start.2
  453.4 4.8 copy-start.4
  453.4 6.8 slice-start.4
  458.2 2.0 slice-start.5
Sparse Core Ops, SparseCore 0:
  9.5 47.1 all-gather.20
  58.9 41.6 all-gather.16
  102.7 40.2 all-gather.14
  207.2 188.1 all-gather.10
  397.3 41.1 all-gather.18
  496.8 178.3 all-gather.12
